TPU v7x, 32 devices: a whole 2x2x4 slice. The times are simulated.
32 devices in a mesh: region: 4 (over y, x), col: 8 (over z, core).
Axes of the slice: x: 2, y: 2, z: 4, core: 2. Of those that a mesh axis runs over, the one named last changes fastest.
Arguments:
- tiles: float32 [1536, 128, 128], P(('region', 'col')), may hold values from -0.109375 to 0.109375
- tile_rows: int32 [1536], P(('region', 'col')), may hold values from 0 to 1
- tile_cols: int32 [1536], P(('region', 'col')), may hold values from 0 to 15
- tile_count: int32 [32], P(('region', 'col')), may hold values from 12 to 48, as said below
- rhs: float32 [64, 128], P(('region', 'col')), may hold values from -6 to 6
- base_cost: float32 [64, 128], P(('region', 'col')), may hold values from 0.1 to 1
- upper: float32 [64, 128], P(('region', 'col')), may hold values from 0.5 to 4
- primal: float32 [64, 16, 128], P(('region', 'col')), may hold values from 0 to 1
- dual: float32 [64, 16, 128], P(('region', 'col')), may hold values from 0 to 1
- price_levels: float32 [32, 128], replicated, may hold values from 0.5 to 2
- scenario_ids: int32 [16], replicated, may hold values from 0 to 31
Outputs:
- primal_out: float32 [64, 16, 128], P(('region', 'col'))
- dual_out: float32 [64, 16, 128], P(('region', 'col'))
- weight_out: float32 [16], replicated
Inputs may be any that keep to these rules, and one draw needn't show every extreme that they name: `tile_count`: slots at or past a device's count are padding and hold no part of the matrix; in every draw some device has all 48 slots live.
All inputs are finite; a program needn't handle non-finite values.
Results may differ from a plain program's by a relative error of at most 0.0001.
Values sent between devices are 32-bit elements; how exact they have to be, the bound alone decides.
No kernel may reach another device: no remote copies, remote signals or barrier semaphores. Data moves between devices by JAX's collectives and lax.ppermute only.
A program may use at most 64 MiB of HBM per device.

v0:
```python
import jax
import jax.numpy as jnp
from jax import lax
from jax.sharding import PartitionSpec as P

ITERS = 2


def local(
    tiles,
    tile_rows,
    tile_cols,
    tile_count,
    rhs,
    base_cost,
    upper,
    primal,
    dual,
    price_levels,
    scenario_ids,
):
    hp = lax.Precision.HIGHEST
    ntiles = tiles.shape[0]
    row_blocks = rhs.shape[0]
    own_blocks = base_cost.shape[0]
    scenarios = primal.shape[1]
    lanes = primal.shape[2]
    region_blocks = own_blocks * lax.axis_size("col")
    devices = lax.axis_size(("region", "col"))
    live = (jnp.arange(ntiles, dtype=jnp.int32) < tile_count[0]).astype(jnp.float32)
    row_select = (tile_rows[:, None] == jnp.arange(row_blocks, dtype=jnp.int32)[None, :]).astype(
        jnp.float32
    )
    row_live = row_select * live[:, None]
    col_select = (tile_cols[:, None] == jnp.arange(region_blocks, dtype=jnp.int32)[None, :]).astype(
        jnp.float32
    )
    col_live = col_select * live[:, None]
    choose = (
        scenario_ids[:, None] == jnp.arange(price_levels.shape[0], dtype=jnp.int32)[None, :]
    ).astype(jnp.float32)
    factor = jnp.dot(choose, price_levels, precision=hp)
    cost = base_cost[:, None, :] * factor[None, :, :]
    local_a = jnp.sum(jnp.sum(tiles * tiles, axis=(1, 2)) * live)
    local_c = jnp.sum(cost * cost, axis=(0, 2))
    local_b = jnp.sum(rhs * rhs)
    sq_a, sq_c, sq_b = lax.psum((local_a, local_c, local_b), ("region", "col"))
    eta = 0.5 / jnp.sqrt(sq_a / (lanes * row_blocks * devices))
    weight = jnp.sqrt(sq_c) / jnp.sqrt(sq_b)
    width = scenarios * lanes
    for step in range(ITERS):
        tau = (eta / weight)[None, :, None]
        sigma = (eta * weight)[None, :, None]
        dual_rows = jnp.dot(row_select, dual.reshape(row_blocks, width), precision=hp).reshape(
            ntiles, scenarios, lanes
        )
        contrib = jnp.einsum("tij,tsi->tsj", tiles, dual_rows, precision=hp)
        flat_terms = contrib.reshape(ntiles, width)
        partial_value = jnp.dot(col_live.T, flat_terms, precision=hp).reshape(
            region_blocks, scenarios, lanes
        )
        grad = lax.psum_scatter(partial_value, "col", scatter_dimension=0, tiled=True)
        new_primal = jnp.clip(primal - tau * (cost - grad), 0.0, upper[:, None, :])
        point = 2.0 * new_primal - primal
        region_point = lax.all_gather(point, "col", axis=0, tiled=True)
        selected = jnp.dot(
            col_select, region_point.reshape(region_blocks, width), precision=hp
        ).reshape(ntiles, scenarios, lanes)
        image = jnp.einsum("tij,tsj->tsi", tiles, selected, precision=hp)
        product = jnp.dot(row_live.T, image.reshape(ntiles, width), precision=hp).reshape(
            row_blocks, scenarios, lanes
        )
        new_dual = jnp.maximum(dual + sigma * (rhs[:, None, :] - product), 0.0)
        local_x = jnp.sum((new_primal - primal) ** 2, axis=(0, 2))
        local_y = jnp.sum((new_dual - dual) ** 2, axis=(0, 2))
        step_x = lax.psum(local_x, ("region", "col"))
        step_y = lax.psum(local_y, ("region", "col"))
        weight = jnp.sqrt(weight * jnp.sqrt((step_x + 1e-06) / (step_y + 1e-06)))
        primal, dual = (new_primal, new_dual)
    return (primal, dual, weight)


def solution(mesh):
    placed = (
        P(("region", "col"), None, None),
        P(("region", "col")),
        P(("region", "col")),
        P(("region", "col")),
        P(("region", "col"), None),
        P(("region", "col"), None),
        P(("region", "col"), None),
        P(("region", "col"), None, None),
        P(("region", "col"), None, None),
        P(),
        P(),
    )
    return jax.shard_map(
        local,
        mesh=mesh,
        in_specs=placed,
        out_specs=(P(("region", "col"), None, None), P(("region", "col"), None, None), P()),
        check_vma=False,
    )
```

profile of v0, /device:TPU:10, one launch (start us, length us, event | category | flops | bytes accessed | tf_op | source)
XLA Modules:
  0.0 194.1 jit_solution(15329960555821616585)
XLA Ops:
  7.2 0.0 copy-start
  7.2 0.0 copy-start.1
  7.2 0.0 copy-start.7
  7.2 0.0 reduce-scatter.3.cloned.1.call-start
  8.1 1.2 fusion.37
  9.3 0.0 copy-start.10
  9.3 0.0 copy-start.5
  9.3 0.0 copy-start.9
  9.3 0.0 copy-start.3
  9.3 0.0 copy-start.8
  9.3 4.7 %fusion.18 = f32[48,16,128]{2,1,0:T(8,128)S(1)} fusion(f32[48,128,128]{2,1,0:T(8,128)} %param.11, f32[48,16,128]{2,0,1:T(8,128)S(1)} %fusion.37), kind=kOutput, calls=%fused_computation.23 | convolution fusion | flops 150994944 | bytes 3932160 | tf_op jit(solution)/shard_map/tij,tsi->tsj/dot_general | solution.py:57
  14.1 0.0 copy-done.7
  14.1 0.4 fusion.9
  14.5 0.7 copy.80
  15.2 0.0 reduce-scatter.3.cloned.1.call-update
  15.2 0.0 reduce-scatter.5.cloned.1.call-start
  15.2 0.0 copy-done.1
  15.3 0.5 multiply_reduce_fusion
  15.7 0.6 fusion.68
  16.3 0.0 copy-done.10
  16.3 0.2 fusion.52
  16.5 0.1 fusion.26
  16.6 0.0 copy-done.9
  16.6 0.6 multiply_reduce_fusion.5
  17.2 41.5 %all-reduce.2 = (f32[16]{0:T(128)S(1)}, f32[]{:T(128)}, f32[]{:T(128)}) all-reduce(f32[16]{0:T(128)S(1)} %fusion.26, f32[]{:T(128)} %fusion.68, f32[]{:T(128)} %multiply_reduce_fusion.5), channel_id=1, replica_groups=mesh['region'=4,'col'=8] {'region','col'}, use_global_device_ids=true, to_apply=%region_6.0 | all-reduce | flops 18 | bytes 144 | tf_op jit(solution)/shard_map/psum | solution.py:47
  60.2 0.0 reduce-scatter.3.cloned.1.call-done
  60.2 0.9 multiply_reduce_fusion.4
  61.1 13.1 %all_gather.6 = f32[16,16,128]{2,1,0:T(8,128)S(1)} all-gather(f32[2,16,128]{2,1,0:T(8,128)S(1)} %multiply_subtract_fusion.3), channel_id=1, replica_groups=mesh['region'=4,'col'=8] {'col'}, dimensions={0}, use_global_device_ids=true | all-gather | bytes 147456 | tf_op jit(solution)/shard_map/all_gather | solution.py:65
  74.2 0.4 fusion.23
  74.6 5.0 %fusion.16 = f32[48,16,128]{2,1,0:T(8,128)S(1)} fusion(f32[48,128,128]{2,1,0:T(8,128)S(1)} %copy-done.1, f32[48,16,128]{2,0,1:T(8,128)S(1)} %fusion.23), kind=kOutput, calls=%fused_computation.21 | convolution fusion | flops 150994944 | bytes 3932160 | tf_op jit(solution)/shard_map/tij,tsj->tsi/dot_general | solution.py:69
  79.5 0.0 copy-done.6
  79.5 0.4 fusion.6
  80.0 0.2 multiply_reduce_fusion.3
  80.2 0.4 fusion.35
  80.6 2.9 %fusion.14 = f32[48,16,128]{2,1,0:T(8,128)S(1)} fusion(f32[48,128,128]{2,1,0:T(8,128)S(1)} %copy-done.1, f32[48,16,128]{2,0,1:T(8,128)S(1)} %fusion.35), kind=kOutput, calls=%fused_computation.19 | convolution fusion | flops 150994944 | bytes 3932160 | tf_op jit(solution)/shard_map/tij,tsi->tsj/dot_general | solution.py:57
  83.4 0.4 fusion.3
  83.9 0.7 copy.87
  84.5 0.0 reduce-scatter.5.cloned.1.call-update
  84.6 40.5 %all-reduce.1 = (f32[16]{0:T(128)S(1)}, f32[16]{0:T(128)S(1)}) all-reduce(f32[16]{0:T(128)S(1)} %get-tuple-element.30, f32[16]{0:T(128)S(1)} %get-tuple-element.28), channel_id=1, replica_groups=mesh['region'=4,'col'=8] {'region','col'}, use_global_device_ids=true, to_apply=%region_11.12 | all-reduce | flops 32 | bytes 256 | tf_op jit(solution)/shard_map/psum | solution.py:77
  125.1 0.0 reduce-scatter.5.cloned.1.call-done
  125.1 0.9 multiply_reduce_fusion.2
  126.0 12.4 %all_gather.7 = f32[16,16,128]{2,1,0:T(8,128)S(1)} all-gather(f32[2,16,128]{2,1,0:T(8,128)S(1)} %multiply_subtract_fusion.2), channel_id=1, replica_groups=mesh['region'=4,'col'=8] {'col'}, dimensions={0}, use_global_device_ids=true | all-gather | bytes 147456 | tf_op jit(solution)/shard_map/all_gather | solution.py:65
  138.4 0.4 fusion.20
  138.8 5.0 %fusion.12 = f32[48,16,128]{2,1,0:T(8,128)S(1)} fusion(f32[48,128,128]{2,1,0:T(8,128)S(1)} %copy-done.1, f32[48,16,128]{2,0,1:T(8,128)S(1)} %fusion.20), kind=kOutput, calls=%fused_computation.17 | convolution fusion | flops 150994944 | bytes 3932160 | tf_op jit(solution)/shard_map/tij,tsj->tsi/dot_general | solution.py:69
  143.8 0.4 fusion
  144.2 0.8 multiply_reduce_fusion.1
  145.0 41.7 %all-reduce = (f32[16]{0:T(128)S(1)}, f32[16]{0:T(128)S(1)}) all-reduce(f32[16]{0:T(128)S(1)} %get-tuple-element.24, f32[16]{0:T(128)S(1)} %get-tuple-element.22), channel_id=1, replica_groups=mesh['region'=4,'col'=8] {'region','col'}, use_global_device_ids=true, to_apply=%region_16.17 | all-reduce | flops 32 | bytes 256 | tf_op jit(solution)/shard_map/psum | solution.py:77
  186.7 0.5 multiply_sqrt_fusion
  (15 shorter events, 0.1 us)
Async XLA Ops:
  7.2 9.2 %copy-start = (f32[32,128]{1,0:T(8,128)S(1)}, f32[32,128]{1,0:T(8,128)}, u32[]{:S(2)}) copy-start(f32[32,128]{1,0:T(8,128)} %param.20) | copy-start | bytes 49156
  7.2 8.1 %copy-start.1 = (f32[48,128,128]{2,1,0:T(8,128)S(1)}, f32[48,128,128]{2,1,0:T(8,128)}, u32[]{:S(2)}) copy-start(f32[48,128,128]{2,1,0:T(8,128)} %param.11) | copy-start | bytes 9437188
  7.2 6.9 %copy-start.7 = (s32[48]{0:T(128)S(1)}, s32[48]{0:T(128)}, u32[]{:S(2)}) copy-start(s32[48]{0:T(128)} %param.13) | copy-start | bytes 580
  7.2 53.0 %reduce-scatter.3.cloned.1.call-start = ((), (), s32[]{:S(2)}) async-start(), calls=%async_computation.2 | async-start | bytes 147456 | tf_op jit(solution)/shard_map/reduce_scatter | solution.py:62
  9.3 7.0 %copy-start.10 = (s32[16]{0:T(128)S(1)}, s32[16]{0:T(128)}, u32[]{:S(2)}) copy-start(s32[16]{0:T(128)} %param.21) | copy-start | bytes 196
  9.3 7.2 %copy-start.5 = (f32[2,128]{1,0:T(2,128)S(1)}, f32[2,128]{1,0:T(2,128)}, u32[]{:S(2)}) copy-start(f32[2,128]{1,0:T(2,128)} %param.16) | copy-start | bytes 3076
  9.3 7.3 %copy-start.9 = (f32[2,128]{1,0:T(2,128)S(1)}, f32[2,128]{1,0:T(2,128)}, u32[]{:S(2)}) copy-start(f32[2,128]{1,0:T(2,128)} %param.15) | copy-start | bytes 3076
  9.3 50.9 %copy-start.3 = (f32[2,16,128]{2,1,0:T(8,128)S(1)}, f32[2,16,128]{2,1,0:T(8,128)}, u32[]{:S(2)}) copy-start(f32[2,16,128]{2,1,0:T(8,128)} %param.18) | copy-start | bytes 49156
  9.3 50.9 %copy-start.8 = (f32[2,128]{1,0:T(2,128)S(1)}, f32[2,128]{1,0:T(2,128)}, u32[]{:S(2)}) copy-start(f32[2,128]{1,0:T(2,128)} %param.17) | copy-start | bytes 3076
  15.2 109.9 %reduce-scatter.5.cloned.1.call-start = ((), (), s32[]{:S(2)}) async-start(), calls=%async_computation.3 | async-start | bytes 147456 | tf_op jit(solution)/shard_map/reduce_scatter | solution.py:62
  15.7 63.8 %copy-start.6 = (s32[48]{0:T(128)S(1)}, s32[48]{0:T(128)}, u32[]{:S(2)}) copy-start(s32[48]{0:T(128)} %param.12) | copy-start | bytes 580
  15.7 64.3 %copy-start.2 = (f32[2,16,128]{2,1,0:T(8,128)S(1)}, f32[2,16,128]{2,1,0:T(8,128)}, u32[]{:S(2)}) copy-start(f32[2,16,128]{2,1,0:T(8,128)} %param.19) | copy-start | bytes 49156
  126.0 61.2 %copy-start.4 = (f32[2,16,128]{2,1,0:T(8,128)}, f32[2,16,128]{2,1,0:T(8,128)S(1)}, u32[]{:S(2)}) copy-start(f32[2,16,128]{2,1,0:T(8,128)S(1)} %get-tuple-element.23) | copy-start | bytes 49156
Sparse Core Ops, SparseCore 0:
  15.3 27.7 reduce-scatter.2
  84.7 26.8 reduce-scatter.4
where the time goes:
time: 195 us; the launch traced here: 194 us
  blocking collectives  149 us (76%)
  matrix products  21.7 us (11%)
  between operations  16.4 us (8%)
  other arithmetic  5.15 us (3%)
    psum x2, blocking collectives, local(): step_y = lax.psum(local_y, ('region', 'col'))  82.2 us
    psum x1, blocking collectives, local(): sq_a, sq_c, sq_b = lax.psum((local_a, local_c, local_b), ('region', 'col'))  41.5 us
    all_gather x2, blocking collectives, local(): region_point = lax.all_gather(point, 'col', axis=0, tiled=True)  25.5 us
    dot_general x2, matrix products, local(): image = jnp.einsum('tij,tsj->tsi', tiles, selected, precision=hp)  9.98 us
    dot_general x2, matrix products, local(): contrib = jnp.einsum('tij,tsi->tsj', tiles, dual_rows, precision=hp)  7.59 us
  transfers between devices with their start and end apart: 2, of which 0 were waited for; matrix products, arithmetic and copies ran while one was open for 1% of the time, Pallas kernels for 0%

commit v1 on v0

--- a/solution.py
+++ b/solution.py
@@ -74,7 +74,7 @@
         local_x = jnp.sum((new_primal - primal) ** 2, axis=(0, 2))
         local_y = jnp.sum((new_dual - dual) ** 2, axis=(0, 2))
         step_x = lax.psum(local_x, ("region", "col"))
-        step_y = lax.psum(local_y, ("region", "col"))
+        step_y = jnp.sum(lax.all_gather(local_y, ("region", "col")), axis=0)
         weight = jnp.sqrt(weight * jnp.sqrt((step_x + 1e-06) / (step_y + 1e-06)))
         primal, dual = (new_primal, new_dual)
     return (primal, dual, weight)

time: 195 us -> 226 us (1.16)
  waiting for transfers between devices: 0.07 us -> 26.5 us
  blocking collectives: 149 us -> 153 us
    unnamed x0 -> x2, blocking collectives: none -> 83.9 us
    psum x2 -> x0, blocking collectives: 82.2 us -> none  [local(): step_y = lax.psum(local_y, ('region', 'col'))]
    reduce_scatter x2, waiting for transfers between devices: 0.04 us -> 26.5 us  [local(): lax.psum_scatter(partial_value, 'col', scatter_dimension=0, tiled=True)]
  transfers between devices with their start and end apart: 2 -> 2, of which waited for: 0 -> 1; matrix products, arithmetic and copies ran while one was open for 1% -> 1% of each run, Pallas kernels for 0% -> 0%
where the time goes in v1:
time: 226 us; the launch traced here: 225 us
  blocking collectives  153 us (68%)
  waiting for transfers between devices  26.5 us (12%)
  matrix products  21.7 us (10%)
  between operations  16.4 us (7%)
  other arithmetic  5.22 us (2%)
    unnamed x2, blocking collectives  83.9 us
    psum x1, blocking collectives, local(): sq_a, sq_c, sq_b = lax.psum((local_a, local_c, local_b), ('region', 'col'))  41.5 us
    all_gather x2, blocking collectives, local(): region_point = lax.all_gather(point, 'col', axis=0, tiled=True)  27.1 us
    reduce_scatter x2, waiting for transfers between devices, local(): lax.psum_scatter(partial_value, 'col', scatter_dimension=0, tiled=True)  26.5 us
    dot_general x2, matrix products, local(): image = jnp.einsum('tij,tsj->tsi', tiles, selected, precision=hp)  9.98 us
    dot_general x2, matrix products, local(): contrib = jnp.einsum('tij,tsi->tsj', tiles, dual_rows, precision=hp)  7.59 us
  transfers between devices with their start and end apart: 2, of which 1 were waited for; matrix products, arithmetic and copies ran while one was open for 1% of the time, Pallas kernels for 0%

profile of v1, /device:TPU:10, one launch (start us, length us, event | category | flops | bytes accessed | tf_op | source)
XLA Modules:
  0.0 224.7 jit_solution(8091654651615297783)
XLA Ops:
  7.2 0.0 copy-start
  7.2 0.0 copy-start.1
  7.2 0.0 copy-start.7
  7.2 0.0 reduce-scatter.3.cloned.1.call-start
  8.1 1.2 fusion.37
  9.3 0.0 copy-start.10
  9.3 0.0 copy-start.5
  9.3 0.0 copy-start.9
  9.3 0.0 copy-start.3
  9.3 0.0 copy-start.8
  9.3 4.7 %fusion.18 = f32[48,16,128]{2,1,0:T(8,128)S(1)} fusion(f32[48,128,128]{2,1,0:T(8,128)} %param.11, f32[48,16,128]{2,0,1:T(8,128)S(1)} %fusion.37), kind=kOutput, calls=%fused_computation.23 | convolution fusion | flops 150994944 | bytes 3932160 | tf_op jit(solution)/shard_map/tij,tsi->tsj/dot_general | solution.py:57
  14.1 0.4 fusion.9
  14.5 0.7 copy.80
  15.2 0.0 reduce-scatter.3.cloned.1.call-update
  15.2 0.0 reduce-scatter.5.cloned.1.call-start
  15.3 0.5 multiply_reduce_fusion
  15.7 0.0 copy-start.2
  15.7 0.2 fusion.52
  15.9 0.1 fusion.26
  16.0 0.6 fusion.68
  16.7 0.6 multiply_reduce_fusion.5
  17.3 41.5 %all-reduce.4 = (f32[16]{0:T(128)S(1)}, f32[]{:T(128)}, f32[]{:T(128)}) all-reduce(f32[16]{0:T(128)S(1)} %fusion.26, f32[]{:T(128)} %fusion.68, f32[]{:T(128)} %multiply_reduce_fusion.5), channel_id=1, replica_groups=mesh['region'=4,'col'=8] {'region','col'}, use_global_device_ids=true, to_apply=%region_6.0 | all-reduce | flops 18 | bytes 144 | tf_op jit(solution)/shard_map/psum | solution.py:47
  60.2 0.0 reduce-scatter.3.cloned.1.call-done
  60.2 0.9 multiply_reduce_fusion.4
  61.2 12.9 %all_gather.18 = f32[16,16,128]{2,1,0:T(8,128)S(1)} all-gather(f32[2,16,128]{2,1,0:T(8,128)S(1)} %multiply_subtract_fusion.3), channel_id=1, replica_groups=mesh['region'=4,'col'=8] {'col'}, dimensions={0}, use_global_device_ids=true | all-gather | bytes 147456 | tf_op jit(solution)/shard_map/all_gather | solution.py:65
  74.0 0.4 fusion.23
  74.4 5.0 %fusion.16 = f32[48,16,128]{2,1,0:T(8,128)S(1)} fusion(f32[48,128,128]{2,1,0:T(8,128)S(1)} %copy-done.1, f32[48,16,128]{2,0,1:T(8,128)S(1)} %fusion.23), kind=kOutput, calls=%fused_computation.21 | convolution fusion | flops 150994944 | bytes 3932160 | tf_op jit(solution)/shard_map/tij,tsj->tsi/dot_general | solution.py:69
  79.4 0.4 fusion.6
  79.8 0.2 multiply_reduce_fusion.3
  80.0 0.2 dynamic-update-slice
  80.2 40.5 %all-reduce.3 = (f32[512]{0:T(512)S(1)}, f32[16]{0:T(128)S(1)}) all-reduce(f32[512]{0:T(512)S(1)} %dynamic-update-slice, f32[16]{0:T(128)S(1)} %get-tuple-element.28), channel_id=2, replica_groups=mesh['region'=4,'col'=8] {'region','col'}, use_global_device_ids=true, to_apply=%add | all-reduce | flops 528 | bytes 4224
  120.8 0.1 reshape.70
  120.9 0.4 fusion.35
  121.2 2.9 %fusion.14 = f32[48,16,128]{2,1,0:T(8,128)S(1)} fusion(f32[48,128,128]{2,1,0:T(8,128)S(1)} %copy-done.1, f32[48,16,128]{2,0,1:T(8,128)S(1)} %fusion.35), kind=kOutput, calls=%fused_computation.19 | convolution fusion | flops 150994944 | bytes 3932160 | tf_op jit(solution)/shard_map/tij,tsi->tsj/dot_general | solution.py:57
  124.1 0.4 fusion.3
  124.5 0.7 copy.87
  125.2 0.0 reduce-scatter.5.cloned.1.call-update
  125.3 26.5 %reduce-scatter.5.cloned.1.call-done = f32[2,16,128]{2,1,0:T(8,128)} async-done(((f32[16,16,128]{2,1,0:T(8,128)}), f32[2,16,128]{2,1,0:T(8,128)}) %reduce-scatter.5.cloned.1.call-update) | async-done | bytes 16400 | tf_op jit(solution)/shard_map/reduce_scatter | solution.py:62
  151.8 0.9 multiply_reduce_fusion.2
  152.7 14.3 %all_gather.21 = f32[16,16,128]{2,1,0:T(8,128)S(1)} all-gather(f32[2,16,128]{2,1,0:T(8,128)S(1)} %multiply_subtract_fusion.2), channel_id=1, replica_groups=mesh['region'=4,'col'=8] {'col'}, dimensions={0}, use_global_device_ids=true | all-gather | bytes 147456 | tf_op jit(solution)/shard_map/all_gather | solution.py:65
  167.0 0.4 fusion.20
  167.3 5.0 %fusion.12 = f32[48,16,128]{2,1,0:T(8,128)S(1)} fusion(f32[48,128,128]{2,1,0:T(8,128)S(1)} %copy-done.1, f32[48,16,128]{2,0,1:T(8,128)S(1)} %fusion.20), kind=kOutput, calls=%fused_computation.17 | convolution fusion | flops 150994944 | bytes 3932160 | tf_op jit(solution)/shard_map/tij,tsj->tsi/dot_general | solution.py:69
  172.3 0.4 fusion
  172.7 0.8 multiply_reduce_fusion.1
  173.5 0.2 dynamic-update-slice.1
  173.8 43.4 %all-reduce.2 = (f32[512]{0:T(512)S(1)}, f32[16]{0:T(128)S(1)}) all-reduce(f32[512]{0:T(512)S(1)} %dynamic-update-slice.1, f32[16]{0:T(128)S(1)} %get-tuple-element.22), channel_id=3, replica_groups=mesh['region'=4,'col'=8] {'region','col'}, use_global_device_ids=true, to_apply=%add.1 | all-reduce | flops 528 | bytes 4224
  217.2 0.1 reshape.71
  217.3 0.5 multiply_sqrt_fusion
  (23 shorter events, 0.1 us)
Async XLA Ops:
  7.2 8.5 %copy-start = (f32[32,128]{1,0:T(8,128)S(1)}, f32[32,128]{1,0:T(8,128)}, u32[]{:S(2)}) copy-start(f32[32,128]{1,0:T(8,128)} %param.20) | copy-start | bytes 49156
  7.2 8.1 %copy-start.1 = (f32[48,128,128]{2,1,0:T(8,128)S(1)}, f32[48,128,128]{2,1,0:T(8,128)}, u32[]{:S(2)}) copy-start(f32[48,128,128]{2,1,0:T(8,128)} %param.11) | copy-start | bytes 9437188
  7.2 6.9 %copy-start.7 = (s32[48]{0:T(128)S(1)}, s32[48]{0:T(128)}, u32[]{:S(2)}) copy-start(s32[48]{0:T(128)} %param.13) | copy-start | bytes 580
  7.2 53.0 %reduce-scatter.3.cloned.1.call-start = ((), (), s32[]{:S(2)}) async-start(), calls=%async_computation.2 | async-start | bytes 147456 | tf_op jit(solution)/shard_map/reduce_scatter | solution.py:62
  9.3 6.4 %copy-start.10 = (s32[16]{0:T(128)S(1)}, s32[16]{0:T(128)}, u32[]{:S(2)}) copy-start(s32[16]{0:T(128)} %param.21) | copy-start | bytes 196
  9.3 6.6 %copy-start.5 = (f32[2,128]{1,0:T(2,128)S(1)}, f32[2,128]{1,0:T(2,128)}, u32[]{:S(2)}) copy-start(f32[2,128]{1,0:T(2,128)} %param.16) | copy-start | bytes 3076
  9.3 7.4 %copy-start.9 = (f32[2,128]{1,0:T(2,128)S(1)}, f32[2,128]{1,0:T(2,128)}, u32[]{:S(2)}) copy-start(f32[2,128]{1,0:T(2,128)} %param.15) | copy-start | bytes 3076
  9.3 50.9 %copy-start.3 = (f32[2,16,128]{2,1,0:T(8,128)S(1)}, f32[2,16,128]{2,1,0:T(8,128)}, u32[]{:S(2)}) copy-start(f32[2,16,128]{2,1,0:T(8,128)} %param.18) | copy-start | bytes 49156
  9.3 50.9 %copy-start.8 = (f32[2,128]{1,0:T(2,128)S(1)}, f32[2,128]{1,0:T(2,128)}, u32[]{:S(2)}) copy-start(f32[2,128]{1,0:T(2,128)} %param.17) | copy-start | bytes 3076
  15.2 136.6 %reduce-scatter.5.cloned.1.call-start = ((), (), s32[]{:S(2)}) async-start(), calls=%async_computation.3 | async-start | bytes 147456 | tf_op jit(solution)/shard_map/reduce_scatter | solution.py:62
  15.7 63.7 %copy-start.6 = (s32[48]{0:T(128)S(1)}, s32[48]{0:T(128)}, u32[]{:S(2)}) copy-start(s32[48]{0:T(128)} %param.12) | copy-start | bytes 580
  15.7 64.1 %copy-start.2 = (f32[2,16,128]{2,1,0:T(8,128)S(1)}, f32[2,16,128]{2,1,0:T(8,128)}, u32[]{:S(2)}) copy-start(f32[2,16,128]{2,1,0:T(8,128)} %param.19) | copy-start | bytes 49156
  152.7 65.1 %copy-start.4 = (f32[2,16,128]{2,1,0:T(8,128)}, f32[2,16,128]{2,1,0:T(8,128)S(1)}, u32[]{:S(2)}) copy-start(f32[2,16,128]{2,1,0:T(8,128)S(1)} %get-tuple-element.23) | copy-start | bytes 49156
Sparse Core Ops, SparseCore 0:
  15.3 27.7 reduce-scatter.2
  125.4 26.3 reduce-scatter.4
